TPU v7x, 32 devices: a whole 2x2x4 slice. The times are simulated.
32 devices in a mesh: tm: 8 (over y, x, core), space: 4 (over z).
Axes of the slice: x: 2, y: 2, z: 4, core: 2. Of those that a mesh axis runs over, the one named last changes fastest.
Arguments:
- starts: float32 [8, 32, 128, 128], P('tm', 'space'), may hold values from -6 to 6
- diffusivity: float32 [32, 128, 128], P('space'), may hold values from 0.04 to 0.2
- velocity: float32 [2, 32, 128, 128], P(None, 'space'), may hold values from -0.1 to 0.1
- obstacle: int32 [32, 128, 128], P('space'), may hold values from 0 to 1, as said below
- substep_scale: float32 [12], replicated, may hold values from 0.5 to 1
- neighbors: int32 [32, 4], P('space'), may hold values from 0 to 32, as said below
- coarse_x: float32 [32, 64, 64], P('space'), may hold values from -1 to 1
- coarse_y: float32 [32, 128, 128], P('space'), may hold values from -1 to 1
Outputs:
- slice_ends: float32 [8, 32, 128, 128], P('tm', 'space')
- increment: float32 [8, 32, 128, 128], P('tm', 'space')
Inputs may be any that keep to these rules, and one draw needn't show every extreme that they name: `neighbors`: tiles form a grid of 4 by 8; each entry names the tile beside a tile in the given direction, or 32 on the grid's edge. The tiles 8 * k to 8 * (k + 1) - 1 fill grid row k, in any order within it, so a neighbour's number differs from the tile's block k by at most one block. `obstacle`: each tile holds one tube, a disc of radius 128 // 8 to 32 cells.
All inputs are finite; a program needn't handle non-finite values.
Results may differ from a plain program's by a relative error of at most 0.0002.
Values sent between devices are 32-bit elements; how exact they have to be, the bound alone decides.
No kernel may reach another device: no remote copies, remote signals or barrier semaphores. Data moves between devices by JAX's collectives and lax.ppermute only.
A program may use at most 128 MiB of HBM per device.

v0:
```python
import jax
import jax.numpy as jnp
from jax import lax
from jax.sharding import PartitionSpec as P

SUB = 12
exact_precision = lax.Precision.HIGHEST


def padded(block, sides, width):
    for axis, dim in sides:
        count = lax.axis_size(axis)
        forward = [(i, i + 1) for i in range(count - 1)]
        backward = [(target, source) for source, target in forward]
        low = lax.ppermute(
            lax.slice_in_dim(block, block.shape[dim] - width, None, axis=dim), axis, forward
        )
        high = lax.ppermute(lax.slice_in_dim(block, 0, width, axis=dim), axis, backward)
        block = jnp.concatenate([low, block, high], axis=dim)
    return block


def spread(value, axis, source):
    kept = jnp.where(lax.axis_index(axis) == source, value, 0).astype(value.dtype)
    return lax.psum(kept, axis)


def passed_along(block, axis, distance):
    devices = range(lax.axis_size(axis))
    route = [(i - distance, i) for i in devices if i - distance in devices]
    return lax.ppermute(block, axis, route)


def restrict(values):
    return 0.5 * (values[..., 0::2, :] + values[..., 1::2, :])


def prolong(coarse_values):
    return jnp.repeat(coarse_values, 2, axis=-2)


def apply_coarse(coarse_values, matrix_x, matrix_y):
    mixed_x = jnp.einsum("tij,...tjk->...tik", matrix_x, coarse_values, precision=exact_precision)
    return jnp.einsum("...tik,tlk->...til", mixed_x, matrix_y, precision=exact_precision)


def on_device(
    starts, diffusivity, velocity, obstacle, substep_scale, neighbors, coarse_x, coarse_y
):
    slice_count = starts.shape[0]
    tile_count = starts.shape[1]
    all_tiles = tile_count * lax.axis_size("space")
    block_base = lax.axis_index("space") * tile_count
    open_cells = 1.0 - obstacle.astype(jnp.float32)
    speed_x = velocity[0]
    speed_y = velocity[1]
    shifted = neighbors - block_base + tile_count
    lookup_index = jnp.where(neighbors == all_tiles, 3 * tile_count, shifted)

    def advance(substep_index, current):
        strength = substep_scale[substep_index]
        own_faces = jnp.stack(
            [current[:, :, 0, :], current[:, :, -1, :], current[:, :, :, 0], current[:, :, :, -1]],
            axis=2,
        )
        gathered = padded(own_faces, (("space", 1),), tile_count)
        gathered = jnp.concatenate([gathered, jnp.zeros_like(gathered[:, :1])], axis=1)
        west_face = gathered[:, lookup_index[:, 0], 1]
        east_face = gathered[:, lookup_index[:, 1], 0]
        south_face = gathered[:, lookup_index[:, 2], 3]
        north_face = gathered[:, lookup_index[:, 3], 2]
        from_west = jnp.concatenate([west_face[:, :, None, :], current[:, :, :-1, :]], axis=2)
        from_east = jnp.concatenate([current[:, :, 1:, :], east_face[:, :, None, :]], axis=2)
        from_south = jnp.concatenate([south_face[:, :, :, None], current[:, :, :, :-1]], axis=3)
        from_north = jnp.concatenate([current[:, :, :, 1:], north_face[:, :, :, None]], axis=3)
        laplace = from_west + from_east + from_south + from_north - 4.0 * current
        transport = speed_x * (from_east - from_west) + speed_y * (from_north - from_south)
        return open_cells * (current + strength * diffusivity * laplace - 0.5 * transport)

    fine_ends = lax.fori_loop(0, SUB, advance, starts)
    correction = fine_ends - prolong(apply_coarse(restrict(starts), coarse_x, coarse_y))
    coarse_jump = restrict(correction)
    first_coarse = spread(restrict(starts[0]), "tm", 0)
    every_jump = lax.all_gather(coarse_jump, "tm", axis=0, tiled=True)

    def sweep(state_now, jump):
        return (apply_coarse(state_now, coarse_x, coarse_y) + jump, state_now)

    last_state, history = lax.scan(sweep, first_coarse, every_jump)
    own_coarse = lax.dynamic_slice_in_dim(
        history, lax.axis_index("tm") * slice_count, slice_count, 0
    )
    slice_ends = prolong(apply_coarse(own_coarse, coarse_x, coarse_y)) + correction
    previous = passed_along(slice_ends[-1], "tm", 1)
    first_step = jnp.where(
        lax.axis_index("tm") == 0, jnp.zeros_like(previous), previous - starts[0]
    )
    increment = jnp.concatenate([first_step[None], slice_ends[:-1] - starts[1:]], axis=0)
    return (slice_ends, increment)


def solution(mesh):
    placed = (
        P("tm", "space", None, None),
        P("space", None, None),
        P(None, "space", None, None),
        P("space", None, None),
        P(),
        P("space", None),
        P("space", None, None),
        P("space", None, None),
    )
    return jax.shard_map(
        on_device,
        mesh=mesh,
        in_specs=placed,
        out_specs=(P("tm", "space", None, None), P("tm", "space", None, None)),
        check_vma=False,
    )
```

profile of v0, /device:TPU:4, one launch (start us, length us, event | category | flops | bytes accessed | tf_op | source)
XLA Modules:
  0.0 285.6 jit_solution(6165159158150083791)
XLA Ops:
  16.3 170.8 %while.25 = (s32[]{:T(128)}, f32[1,8,128,128]{2,1,3,0:T(8,128)S(1)}, f32[8,128,128]{1,0,2:T(8,128)}, f32[12]{0:T(128)S(1)}, f32[8,128,128]{1,0,2:T(8,128)}, /*in...) while((s32[]{:T(128)}, ...), condition=%wide.region_2.3_spmd, body=%wide.region_1.2_spmd.sunk | while | flops 2710714 | bytes 10800037 | solution.py:80
  16.6 3.5 %collective-permute-start.1 = (f32[1,8,4,128]{3,2,1,0:T(4,128)S(1)}, f32[1,8,4,128]{3,2,1,0:T(4,128)S(1)}, u32[]{:S(2)}, u32[]{:S(2)}) collective-permute-start(f32[1,8,4,128]{3,2,1,0:T(4,128)S(1)} %pad_maximum_fusion.6), channel_id=1, source_target_pairs={{0,1},{1,2},{2,3},{4,5},{5,6},{6,7},{8,9},{9,10},{10,11},{12,13},{... | collective-permute-start | bytes 49160 | tf_op jit(solution)/shard_map/while/body/eval_jaxpr/ppermute | solution.py:15
  23.1 2.6 collective-permute-done
  28.7 3.0 %fusion.60 = f32[1,8,128,128]{2,1,3,0:T(8,128)S(1)} fusion(f32[1,8,128,128]{2,1,3,0:T(8,128)S(1)} %get-tuple-element.355, f32[8,128,128]{1,0,2:T(8,128)} %get-tuple-element.367, f32[1,8,128,128]{2,1,3,0:T(8,128)} %get-tuple-element.372, f32[1,8,128,128]{2,1,3,0:T(8,128)} %get-tuple-element.371, f32[1,8,128,1]{2,1,3,0:T(8,128)S(1)} %bitcast.113, ...), kind=kLoop, calls=%fused_computation.13.clone.1 | loop fusion | flops 2621440 | bytes 5242884 | tf_op jit(solution)/shard_map/while/body/eval_jaxpr/mul | solution.py:78
  31.9 3.5 %collective-permute-start.1 = (f32[1,8,4,128]{3,2,1,0:T(4,128)S(1)}, f32[1,8,4,128]{3,2,1,0:T(4,128)S(1)}, u32[]{:S(2)}, u32[]{:S(2)}) collective-permute-start(f32[1,8,4,128]{3,2,1,0:T(4,128)S(1)} %pad_maximum_fusion.6), channel_id=1, source_target_pairs={{0,1},{1,2},{2,3},{4,5},{5,6},{6,7},{8,9},{9,10},{10,11},{12,13},{... | collective-permute-start | bytes 49160 | tf_op jit(solution)/shard_map/while/body/eval_jaxpr/ppermute | solution.py:15
  38.5 2.6 collective-permute-done
  44.0 3.0 %fusion.60 = f32[1,8,128,128]{2,1,3,0:T(8,128)S(1)} fusion(f32[1,8,128,128]{2,1,3,0:T(8,128)S(1)} %get-tuple-element.355, f32[8,128,128]{1,0,2:T(8,128)} %get-tuple-element.367, f32[1,8,128,128]{2,1,3,0:T(8,128)} %get-tuple-element.372, f32[1,8,128,128]{2,1,3,0:T(8,128)} %get-tuple-element.371, f32[1,8,128,1]{2,1,3,0:T(8,128)S(1)} %bitcast.113, ...), kind=kLoop, calls=%fused_computation.13.clone.1 | loop fusion | flops 2621440 | bytes 5242884 | tf_op jit(solution)/shard_map/while/body/eval_jaxpr/mul | solution.py:78
  47.3 3.5 %collective-permute-start.1 = (f32[1,8,4,128]{3,2,1,0:T(4,128)S(1)}, f32[1,8,4,128]{3,2,1,0:T(4,128)S(1)}, u32[]{:S(2)}, u32[]{:S(2)}) collective-permute-start(f32[1,8,4,128]{3,2,1,0:T(4,128)S(1)} %pad_maximum_fusion.6), channel_id=1, source_target_pairs={{0,1},{1,2},{2,3},{4,5},{5,6},{6,7},{8,9},{9,10},{10,11},{12,13},{... | collective-permute-start | bytes 49160 | tf_op jit(solution)/shard_map/while/body/eval_jaxpr/ppermute | solution.py:15
  53.9 2.6 collective-permute-done
  59.4 3.0 %fusion.60 = f32[1,8,128,128]{2,1,3,0:T(8,128)S(1)} fusion(f32[1,8,128,128]{2,1,3,0:T(8,128)S(1)} %get-tuple-element.355, f32[8,128,128]{1,0,2:T(8,128)} %get-tuple-element.367, f32[1,8,128,128]{2,1,3,0:T(8,128)} %get-tuple-element.372, f32[1,8,128,128]{2,1,3,0:T(8,128)} %get-tuple-element.371, f32[1,8,128,1]{2,1,3,0:T(8,128)S(1)} %bitcast.113, ...), kind=kLoop, calls=%fused_computation.13.clone.1 | loop fusion | flops 2621440 | bytes 5242884 | tf_op jit(solution)/shard_map/while/body/eval_jaxpr/mul | solution.py:78
  62.7 2.0 collective-permute-start.1
  67.7 2.6 collective-permute-done
  73.3 3.0 %fusion.60 = f32[1,8,128,128]{2,1,3,0:T(8,128)S(1)} fusion(f32[1,8,128,128]{2,1,3,0:T(8,128)S(1)} %get-tuple-element.355, f32[8,128,128]{1,0,2:T(8,128)} %get-tuple-element.367, f32[1,8,128,128]{2,1,3,0:T(8,128)} %get-tuple-element.372, f32[1,8,128,128]{2,1,3,0:T(8,128)} %get-tuple-element.371, f32[1,8,128,1]{2,1,3,0:T(8,128)S(1)} %bitcast.113, ...), kind=kLoop, calls=%fused_computation.13.clone.1 | loop fusion | flops 2621440 | bytes 5242884 | tf_op jit(solution)/shard_map/while/body/eval_jaxpr/mul | solution.py:78
  81.6 2.6 collective-permute-done
  87.1 3.0 %fusion.60 = f32[1,8,128,128]{2,1,3,0:T(8,128)S(1)} fusion(f32[1,8,128,128]{2,1,3,0:T(8,128)S(1)} %get-tuple-element.355, f32[8,128,128]{1,0,2:T(8,128)} %get-tuple-element.367, f32[1,8,128,128]{2,1,3,0:T(8,128)} %get-tuple-element.372, f32[1,8,128,128]{2,1,3,0:T(8,128)} %get-tuple-element.371, f32[1,8,128,1]{2,1,3,0:T(8,128)S(1)} %bitcast.113, ...), kind=kLoop, calls=%fused_computation.13.clone.1 | loop fusion | flops 2621440 | bytes 5242884 | tf_op jit(solution)/shard_map/while/body/eval_jaxpr/mul | solution.py:78
  90.4 2.0 collective-permute-start.1
  95.5 2.6 collective-permute-done
  101.0 3.0 %fusion.60 = f32[1,8,128,128]{2,1,3,0:T(8,128)S(1)} fusion(f32[1,8,128,128]{2,1,3,0:T(8,128)S(1)} %get-tuple-element.355, f32[8,128,128]{1,0,2:T(8,128)} %get-tuple-element.367, f32[1,8,128,128]{2,1,3,0:T(8,128)} %get-tuple-element.372, f32[1,8,128,128]{2,1,3,0:T(8,128)} %get-tuple-element.371, f32[1,8,128,1]{2,1,3,0:T(8,128)S(1)} %bitcast.113, ...), kind=kLoop, calls=%fused_computation.13.clone.1 | loop fusion | flops 2621440 | bytes 5242884 | tf_op jit(solution)/shard_map/while/body/eval_jaxpr/mul | solution.py:78
  104.3 2.0 collective-permute-start.1
  109.3 2.6 collective-permute-done
  114.9 3.0 %fusion.60 = f32[1,8,128,128]{2,1,3,0:T(8,128)S(1)} fusion(f32[1,8,128,128]{2,1,3,0:T(8,128)S(1)} %get-tuple-element.355, f32[8,128,128]{1,0,2:T(8,128)} %get-tuple-element.367, f32[1,8,128,128]{2,1,3,0:T(8,128)} %get-tuple-element.372, f32[1,8,128,128]{2,1,3,0:T(8,128)} %get-tuple-element.371, f32[1,8,128,1]{2,1,3,0:T(8,128)S(1)} %bitcast.113, ...), kind=kLoop, calls=%fused_computation.13.clone.1 | loop fusion | flops 2621440 | bytes 5242884 | tf_op jit(solution)/shard_map/while/body/eval_jaxpr/mul | solution.py:78
  118.1 2.0 collective-permute-start.1
  123.2 2.6 collective-permute-done
  128.7 3.0 %fusion.60 = f32[1,8,128,128]{2,1,3,0:T(8,128)S(1)} fusion(f32[1,8,128,128]{2,1,3,0:T(8,128)S(1)} %get-tuple-element.355, f32[8,128,128]{1,0,2:T(8,128)} %get-tuple-element.367, f32[1,8,128,128]{2,1,3,0:T(8,128)} %get-tuple-element.372, f32[1,8,128,128]{2,1,3,0:T(8,128)} %get-tuple-element.371, f32[1,8,128,1]{2,1,3,0:T(8,128)S(1)} %bitcast.113, ...), kind=kLoop, calls=%fused_computation.13.clone.1 | loop fusion | flops 2621440 | bytes 5242884 | tf_op jit(solution)/shard_map/while/body/eval_jaxpr/mul | solution.py:78
  132.0 2.0 collective-permute-start.1
  137.0 2.6 collective-permute-done
  142.6 3.0 %fusion.60 = f32[1,8,128,128]{2,1,3,0:T(8,128)S(1)} fusion(f32[1,8,128,128]{2,1,3,0:T(8,128)S(1)} %get-tuple-element.355, f32[8,128,128]{1,0,2:T(8,128)} %get-tuple-element.367, f32[1,8,128,128]{2,1,3,0:T(8,128)} %get-tuple-element.372, f32[1,8,128,128]{2,1,3,0:T(8,128)} %get-tuple-element.371, f32[1,8,128,1]{2,1,3,0:T(8,128)S(1)} %bitcast.113, ...), kind=kLoop, calls=%fused_computation.13.clone.1 | loop fusion | flops 2621440 | bytes 5242884 | tf_op jit(solution)/shard_map/while/body/eval_jaxpr/mul | solution.py:78
  145.8 2.0 collective-permute-start.1
  150.9 2.6 collective-permute-done
  156.4 3.0 %fusion.60 = f32[1,8,128,128]{2,1,3,0:T(8,128)S(1)} fusion(f32[1,8,128,128]{2,1,3,0:T(8,128)S(1)} %get-tuple-element.355, f32[8,128,128]{1,0,2:T(8,128)} %get-tuple-element.367, f32[1,8,128,128]{2,1,3,0:T(8,128)} %get-tuple-element.372, f32[1,8,128,128]{2,1,3,0:T(8,128)} %get-tuple-element.371, f32[1,8,128,1]{2,1,3,0:T(8,128)S(1)} %bitcast.113, ...), kind=kLoop, calls=%fused_computation.13.clone.1 | loop fusion | flops 2621440 | bytes 5242884 | tf_op jit(solution)/shard_map/while/body/eval_jaxpr/mul | solution.py:78
  159.7 2.0 collective-permute-start.1
  164.8 2.6 collective-permute-done
  170.3 3.0 %fusion.60 = f32[1,8,128,128]{2,1,3,0:T(8,128)S(1)} fusion(f32[1,8,128,128]{2,1,3,0:T(8,128)S(1)} %get-tuple-element.355, f32[8,128,128]{1,0,2:T(8,128)} %get-tuple-element.367, f32[1,8,128,128]{2,1,3,0:T(8,128)} %get-tuple-element.372, f32[1,8,128,128]{2,1,3,0:T(8,128)} %get-tuple-element.371, f32[1,8,128,1]{2,1,3,0:T(8,128)S(1)} %bitcast.113, ...), kind=kLoop, calls=%fused_computation.13.clone.1 | loop fusion | flops 2621440 | bytes 5242884 | tf_op jit(solution)/shard_map/while/body/eval_jaxpr/mul | solution.py:78
  173.6 2.0 collective-permute-start.1
  178.6 2.6 collective-permute-done
  184.2 3.0 %fusion.60 = f32[1,8,128,128]{2,1,3,0:T(8,128)S(1)} fusion(f32[1,8,128,128]{2,1,3,0:T(8,128)S(1)} %get-tuple-element.355, f32[8,128,128]{1,0,2:T(8,128)} %get-tuple-element.367, f32[1,8,128,128]{2,1,3,0:T(8,128)} %get-tuple-element.372, f32[1,8,128,128]{2,1,3,0:T(8,128)} %get-tuple-element.371, f32[1,8,128,1]{2,1,3,0:T(8,128)S(1)} %bitcast.113, ...), kind=kLoop, calls=%fused_computation.13.clone.1 | loop fusion | flops 2621440 | bytes 5242884 | tf_op jit(solution)/shard_map/while/body/eval_jaxpr/mul | solution.py:78
  191.3 26.0 %all-gather.2.cloned.1.call-done = f32[8,8,64,128]{3,2,1,0:T(8,128)} async-done(((f32[1,8,64,128]{3,2,1,0:T(8,128)}), f32[8,8,64,128]{3,2,1,0:T(8,128)}) %all-gather.2.cloned.1.call-update) | async-done | bytes 2097168 | tf_op jit(solution)/shard_map/all_gather | solution.py:84
  217.2 46.5 %while.26 = (s32[]{:T(128)}, f32[8,64,128]{2,1,0:T(8,128)}, f32[8,8,64,128]{3,2,1,0:T(8,128)}, f32[8,64,64]{2,1,0:T(8,128)S(1)}, f32[8,128,128]{2,1,0:T(8,128)S(1)}, /*index=5*/f32[8,8,64,128]{3,2,1,0:T(8,128)}, s32[]{:T(128)}) while((s32[]{:T(128)}, f32[8,64,128]{2,1,0:T(8,128)}, f32[8,8,64,128]{3,2,1,0:T(8,128)}, ...), condition=%wide.region_4.5_spmd, body=%wide.region_3.4_spmd.sunk | while | flops 151060480 | bytes 2490461 | solution.py:89
  220.3 2.8 convolution_add_fusion.2
  226.1 2.8 convolution_add_fusion.2
  231.9 2.8 convolution_add_fusion.2
  237.7 2.8 convolution_add_fusion.2
  243.5 2.8 convolution_add_fusion.2
  249.3 2.8 convolution_add_fusion.2
  255.1 2.8 convolution_add_fusion.2
  260.9 2.8 convolution_add_fusion.2
  266.5 2.1 collective-permute-start.2
  268.6 9.3 %collective-permute-done.2 = f32[8,128,128]{2,1,0:T(8,128)S(1)} collective-permute-done((f32[8,128,128]{2,1,0:T(8,128)S(1)}, f32[8,128,128]{2,1,0:T(8,128)S(1)}, u32[]{:S(2)}, u32[]{:S(2)}) %collective-permute-start.2) | collective-permute-done | bytes 524320 | tf_op jit(solution)/shard_map/ppermute | solution.py:31
  (285 shorter events, 117.6 us)
Async XLA Ops:
  7.2 3.1 %copy-start.2 = (f32[1,8,128,128]{3,2,1,0:T(8,128)S(1)}, f32[1,8,128,128]{3,2,1,0:T(8,128)}, u32[]{:S(2)}) copy-start(f32[1,8,128,128]{3,2,1,0:T(8,128)} %param.12) | copy-start | bytes 1572868
  7.2 184.1 %all-reduce.6.cloned.1.call-start = ((), (), s32[]{:S(2)}) async-start(), calls=%async_computation | async-start | bytes 524288 | tf_op jit(solution)/shard_map/psum | solution.py:25
  7.2 4.8 %copy-start.6 = (f32[8,128,128]{2,1,0:T(8,128)S(1)}, f32[8,128,128]{2,1,0:T(8,128)}, u32[]{:S(2)}) copy-start(f32[8,128,128]{2,1,0:T(8,128)} %param.13) | copy-start | bytes 1572868
  9.4 3.6 %copy-start.7 = (s32[8,128,128]{2,1,0:T(8,128)S(1)}, s32[8,128,128]{2,1,0:T(8,128)}, u32[]{:S(2)}) copy-start(s32[8,128,128]{2,1,0:T(8,128)} %param.15) | copy-start | bytes 1572868
  10.2 207.0 %all-gather.2.cloned.1.call-start = ((), (), s32[]{:S(2)}) async-start(), calls=%async_computation.1 | async-start | bytes 2359296 | tf_op jit(solution)/shard_map/all_gather | solution.py:84
  11.8 2.3 copy-start.4
  14.1 2.1 copy-start.8
  14.1 2.1 copy-start.9
  16.3 171.1 %copy-start.1 = (f32[8,64,64]{2,1,0:T(8,128)S(1)}, f32[8,64,64]{2,1,0:T(8,128)}, u32[]{:S(2)}) copy-start(f32[8,64,64]{2,1,0:T(8,128)} %param.18) | copy-start | bytes 393220
  16.6 6.6 %collective-permute-start.1 = (f32[1,8,4,128]{3,2,1,0:T(4,128)S(1)}, f32[1,8,4,128]{3,2,1,0:T(4,128)S(1)}, u32[]{:S(2)}, u32[]{:S(2)}) collective-permute-start(f32[1,8,4,128]{3,2,1,0:T(4,128)S(1)} %pad_maximum_fusion.6), channel_id=1, source_target_pairs={{0,1},{1,2},{2,3},{4,5},{5,6},{6,7},{8,9},{9,10},{10,11},{12,13},{... | collective-permute-start | bytes 49160 | tf_op jit(solution)/shard_map/while/body/eval_jaxpr/ppermute | solution.py:15
  20.1 5.6 %collective-permute-start = (f32[1,8,4,128]{3,2,1,0:T(4,128)S(1)}, f32[1,8,4,128]{3,2,1,0:T(4,128)S(1)}, u32[]{:S(2)}, u32[]{:S(2)}) collective-permute-start(f32[1,8,4,128]{3,2,1,0:T(4,128)S(1)} %pad_maximum_fusion.6), channel_id=1, source_target_pairs={{1,0},{2,1},{3,2},{5,4},{6,5},{7,6},{9,8},{10,9},{11,10},{13,12},{... | collective-permute-start | bytes 49160 | tf_op jit(solution)/shard_map/while/body/eval_jaxpr/ppermute | solution.py:18
  31.9 6.6 %collective-permute-start.1 = (f32[1,8,4,128]{3,2,1,0:T(4,128)S(1)}, f32[1,8,4,128]{3,2,1,0:T(4,128)S(1)}, u32[]{:S(2)}, u32[]{:S(2)}) collective-permute-start(f32[1,8,4,128]{3,2,1,0:T(4,128)S(1)} %pad_maximum_fusion.6), channel_id=1, source_target_pairs={{0,1},{1,2},{2,3},{4,5},{5,6},{6,7},{8,9},{9,10},{10,11},{12,13},{... | collective-permute-start | bytes 49160 | tf_op jit(solution)/shard_map/while/body/eval_jaxpr/ppermute | solution.py:15
  35.4 5.6 %collective-permute-start = (f32[1,8,4,128]{3,2,1,0:T(4,128)S(1)}, f32[1,8,4,128]{3,2,1,0:T(4,128)S(1)}, u32[]{:S(2)}, u32[]{:S(2)}) collective-permute-start(f32[1,8,4,128]{3,2,1,0:T(4,128)S(1)} %pad_maximum_fusion.6), channel_id=1, source_target_pairs={{1,0},{2,1},{3,2},{5,4},{6,5},{7,6},{9,8},{10,9},{11,10},{13,12},{... | collective-permute-start | bytes 49160 | tf_op jit(solution)/shard_map/while/body/eval_jaxpr/ppermute | solution.py:18
  47.3 6.6 %collective-permute-start.1 = (f32[1,8,4,128]{3,2,1,0:T(4,128)S(1)}, f32[1,8,4,128]{3,2,1,0:T(4,128)S(1)}, u32[]{:S(2)}, u32[]{:S(2)}) collective-permute-start(f32[1,8,4,128]{3,2,1,0:T(4,128)S(1)} %pad_maximum_fusion.6), channel_id=1, source_target_pairs={{0,1},{1,2},{2,3},{4,5},{5,6},{6,7},{8,9},{9,10},{10,11},{12,13},{... | collective-permute-start | bytes 49160 | tf_op jit(solution)/shard_map/while/body/eval_jaxpr/ppermute | solution.py:15
  50.8 5.6 %collective-permute-start = (f32[1,8,4,128]{3,2,1,0:T(4,128)S(1)}, f32[1,8,4,128]{3,2,1,0:T(4,128)S(1)}, u32[]{:S(2)}, u32[]{:S(2)}) collective-permute-start(f32[1,8,4,128]{3,2,1,0:T(4,128)S(1)} %pad_maximum_fusion.6), channel_id=1, source_target_pairs={{1,0},{2,1},{3,2},{5,4},{6,5},{7,6},{9,8},{10,9},{11,10},{13,12},{... | collective-permute-start | bytes 49160 | tf_op jit(solution)/shard_map/while/body/eval_jaxpr/ppermute | solution.py:18
  62.7 5.1 %collective-permute-start.1 = (f32[1,8,4,128]{3,2,1,0:T(4,128)S(1)}, f32[1,8,4,128]{3,2,1,0:T(4,128)S(1)}, u32[]{:S(2)}, u32[]{:S(2)}) collective-permute-start(f32[1,8,4,128]{3,2,1,0:T(4,128)S(1)} %pad_maximum_fusion.6), channel_id=1, source_target_pairs={{0,1},{1,2},{2,3},{4,5},{5,6},{6,7},{8,9},{9,10},{10,11},{12,13},{... | collective-permute-start | bytes 49160 | tf_op jit(solution)/shard_map/while/body/eval_jaxpr/ppermute | solution.py:15
  64.7 5.6 %collective-permute-start = (f32[1,8,4,128]{3,2,1,0:T(4,128)S(1)}, f32[1,8,4,128]{3,2,1,0:T(4,128)S(1)}, u32[]{:S(2)}, u32[]{:S(2)}) collective-permute-start(f32[1,8,4,128]{3,2,1,0:T(4,128)S(1)} %pad_maximum_fusion.6), channel_id=1, source_target_pairs={{1,0},{2,1},{3,2},{5,4},{6,5},{7,6},{9,8},{10,9},{11,10},{13,12},{... | collective-permute-start | bytes 49160 | tf_op jit(solution)/shard_map/while/body/eval_jaxpr/ppermute | solution.py:18
  76.5 5.1 %collective-permute-start.1 = (f32[1,8,4,128]{3,2,1,0:T(4,128)S(1)}, f32[1,8,4,128]{3,2,1,0:T(4,128)S(1)}, u32[]{:S(2)}, u32[]{:S(2)}) collective-permute-start(f32[1,8,4,128]{3,2,1,0:T(4,128)S(1)} %pad_maximum_fusion.6), channel_id=1, source_target_pairs={{0,1},{1,2},{2,3},{4,5},{5,6},{6,7},{8,9},{9,10},{10,11},{12,13},{... | collective-permute-start | bytes 49160 | tf_op jit(solution)/shard_map/while/body/eval_jaxpr/ppermute | solution.py:15
  78.5 5.6 %collective-permute-start = (f32[1,8,4,128]{3,2,1,0:T(4,128)S(1)}, f32[1,8,4,128]{3,2,1,0:T(4,128)S(1)}, u32[]{:S(2)}, u32[]{:S(2)}) collective-permute-start(f32[1,8,4,128]{3,2,1,0:T(4,128)S(1)} %pad_maximum_fusion.6), channel_id=1, source_target_pairs={{1,0},{2,1},{3,2},{5,4},{6,5},{7,6},{9,8},{10,9},{11,10},{13,12},{... | collective-permute-start | bytes 49160 | tf_op jit(solution)/shard_map/while/body/eval_jaxpr/ppermute | solution.py:18
  90.4 5.1 %collective-permute-start.1 = (f32[1,8,4,128]{3,2,1,0:T(4,128)S(1)}, f32[1,8,4,128]{3,2,1,0:T(4,128)S(1)}, u32[]{:S(2)}, u32[]{:S(2)}) collective-permute-start(f32[1,8,4,128]{3,2,1,0:T(4,128)S(1)} %pad_maximum_fusion.6), channel_id=1, source_target_pairs={{0,1},{1,2},{2,3},{4,5},{5,6},{6,7},{8,9},{9,10},{10,11},{12,13},{... | collective-permute-start | bytes 49160 | tf_op jit(solution)/shard_map/while/body/eval_jaxpr/ppermute | solution.py:15
  92.4 5.6 %collective-permute-start = (f32[1,8,4,128]{3,2,1,0:T(4,128)S(1)}, f32[1,8,4,128]{3,2,1,0:T(4,128)S(1)}, u32[]{:S(2)}, u32[]{:S(2)}) collective-permute-start(f32[1,8,4,128]{3,2,1,0:T(4,128)S(1)} %pad_maximum_fusion.6), channel_id=1, source_target_pairs={{1,0},{2,1},{3,2},{5,4},{6,5},{7,6},{9,8},{10,9},{11,10},{13,12},{... | collective-permute-start | bytes 49160 | tf_op jit(solution)/shard_map/while/body/eval_jaxpr/ppermute | solution.py:18
  104.3 5.1 %collective-permute-start.1 = (f32[1,8,4,128]{3,2,1,0:T(4,128)S(1)}, f32[1,8,4,128]{3,2,1,0:T(4,128)S(1)}, u32[]{:S(2)}, u32[]{:S(2)}) collective-permute-start(f32[1,8,4,128]{3,2,1,0:T(4,128)S(1)} %pad_maximum_fusion.6), channel_id=1, source_target_pairs={{0,1},{1,2},{2,3},{4,5},{5,6},{6,7},{8,9},{9,10},{10,11},{12,13},{... | collective-permute-start | bytes 49160 | tf_op jit(solution)/shard_map/while/body/eval_jaxpr/ppermute | solution.py:15
  106.3 5.6 %collective-permute-start = (f32[1,8,4,128]{3,2,1,0:T(4,128)S(1)}, f32[1,8,4,128]{3,2,1,0:T(4,128)S(1)}, u32[]{:S(2)}, u32[]{:S(2)}) collective-permute-start(f32[1,8,4,128]{3,2,1,0:T(4,128)S(1)} %pad_maximum_fusion.6), channel_id=1, source_target_pairs={{1,0},{2,1},{3,2},{5,4},{6,5},{7,6},{9,8},{10,9},{11,10},{13,12},{... | collective-permute-start | bytes 49160 | tf_op jit(solution)/shard_map/while/body/eval_jaxpr/ppermute | solution.py:18
  118.1 5.1 %collective-permute-start.1 = (f32[1,8,4,128]{3,2,1,0:T(4,128)S(1)}, f32[1,8,4,128]{3,2,1,0:T(4,128)S(1)}, u32[]{:S(2)}, u32[]{:S(2)}) collective-permute-start(f32[1,8,4,128]{3,2,1,0:T(4,128)S(1)} %pad_maximum_fusion.6), channel_id=1, source_target_pairs={{0,1},{1,2},{2,3},{4,5},{5,6},{6,7},{8,9},{9,10},{10,11},{12,13},{... | collective-permute-start | bytes 49160 | tf_op jit(solution)/shard_map/while/body/eval_jaxpr/ppermute | solution.py:15
  120.1 5.6 %collective-permute-start = (f32[1,8,4,128]{3,2,1,0:T(4,128)S(1)}, f32[1,8,4,128]{3,2,1,0:T(4,128)S(1)}, u32[]{:S(2)}, u32[]{:S(2)}) collective-permute-start(f32[1,8,4,128]{3,2,1,0:T(4,128)S(1)} %pad_maximum_fusion.6), channel_id=1, source_target_pairs={{1,0},{2,1},{3,2},{5,4},{6,5},{7,6},{9,8},{10,9},{11,10},{13,12},{... | collective-permute-start | bytes 49160 | tf_op jit(solution)/shard_map/while/body/eval_jaxpr/ppermute | solution.py:18
  132.0 5.1 %collective-permute-start.1 = (f32[1,8,4,128]{3,2,1,0:T(4,128)S(1)}, f32[1,8,4,128]{3,2,1,0:T(4,128)S(1)}, u32[]{:S(2)}, u32[]{:S(2)}) collective-permute-start(f32[1,8,4,128]{3,2,1,0:T(4,128)S(1)} %pad_maximum_fusion.6), channel_id=1, source_target_pairs={{0,1},{1,2},{2,3},{4,5},{5,6},{6,7},{8,9},{9,10},{10,11},{12,13},{... | collective-permute-start | bytes 49160 | tf_op jit(solution)/shard_map/while/body/eval_jaxpr/ppermute | solution.py:15
  134.0 5.6 %collective-permute-start = (f32[1,8,4,128]{3,2,1,0:T(4,128)S(1)}, f32[1,8,4,128]{3,2,1,0:T(4,128)S(1)}, u32[]{:S(2)}, u32[]{:S(2)}) collective-permute-start(f32[1,8,4,128]{3,2,1,0:T(4,128)S(1)} %pad_maximum_fusion.6), channel_id=1, source_target_pairs={{1,0},{2,1},{3,2},{5,4},{6,5},{7,6},{9,8},{10,9},{11,10},{13,12},{... | collective-permute-start | bytes 49160 | tf_op jit(solution)/shard_map/while/body/eval_jaxpr/ppermute | solution.py:18
  145.8 5.1 %collective-permute-start.1 = (f32[1,8,4,128]{3,2,1,0:T(4,128)S(1)}, f32[1,8,4,128]{3,2,1,0:T(4,128)S(1)}, u32[]{:S(2)}, u32[]{:S(2)}) collective-permute-start(f32[1,8,4,128]{3,2,1,0:T(4,128)S(1)} %pad_maximum_fusion.6), channel_id=1, source_target_pairs={{0,1},{1,2},{2,3},{4,5},{5,6},{6,7},{8,9},{9,10},{10,11},{12,13},{... | collective-permute-start | bytes 49160 | tf_op jit(solution)/shard_map/while/body/eval_jaxpr/ppermute | solution.py:15
  147.8 5.6 %collective-permute-start = (f32[1,8,4,128]{3,2,1,0:T(4,128)S(1)}, f32[1,8,4,128]{3,2,1,0:T(4,128)S(1)}, u32[]{:S(2)}, u32[]{:S(2)}) collective-permute-start(f32[1,8,4,128]{3,2,1,0:T(4,128)S(1)} %pad_maximum_fusion.6), channel_id=1, source_target_pairs={{1,0},{2,1},{3,2},{5,4},{6,5},{7,6},{9,8},{10,9},{11,10},{13,12},{... | collective-permute-start | bytes 49160 | tf_op jit(solution)/shard_map/while/body/eval_jaxpr/ppermute | solution.py:18
  159.7 5.1 %collective-permute-start.1 = (f32[1,8,4,128]{3,2,1,0:T(4,128)S(1)}, f32[1,8,4,128]{3,2,1,0:T(4,128)S(1)}, u32[]{:S(2)}, u32[]{:S(2)}) collective-permute-start(f32[1,8,4,128]{3,2,1,0:T(4,128)S(1)} %pad_maximum_fusion.6), channel_id=1, source_target_pairs={{0,1},{1,2},{2,3},{4,5},{5,6},{6,7},{8,9},{9,10},{10,11},{12,13},{... | collective-permute-start | bytes 49160 | tf_op jit(solution)/shard_map/while/body/eval_jaxpr/ppermute | solution.py:15
  161.7 5.6 %collective-permute-start = (f32[1,8,4,128]{3,2,1,0:T(4,128)S(1)}, f32[1,8,4,128]{3,2,1,0:T(4,128)S(1)}, u32[]{:S(2)}, u32[]{:S(2)}) collective-permute-start(f32[1,8,4,128]{3,2,1,0:T(4,128)S(1)} %pad_maximum_fusion.6), channel_id=1, source_target_pairs={{1,0},{2,1},{3,2},{5,4},{6,5},{7,6},{9,8},{10,9},{11,10},{13,12},{... | collective-permute-start | bytes 49160 | tf_op jit(solution)/shard_map/while/body/eval_jaxpr/ppermute | solution.py:18
  173.6 5.1 %collective-permute-start.1 = (f32[1,8,4,128]{3,2,1,0:T(4,128)S(1)}, f32[1,8,4,128]{3,2,1,0:T(4,128)S(1)}, u32[]{:S(2)}, u32[]{:S(2)}) collective-permute-start(f32[1,8,4,128]{3,2,1,0:T(4,128)S(1)} %pad_maximum_fusion.6), channel_id=1, source_target_pairs={{0,1},{1,2},{2,3},{4,5},{5,6},{6,7},{8,9},{9,10},{10,11},{12,13},{... | collective-permute-start | bytes 49160 | tf_op jit(solution)/shard_map/while/body/eval_jaxpr/ppermute | solution.py:15
  175.6 5.6 %collective-permute-start = (f32[1,8,4,128]{3,2,1,0:T(4,128)S(1)}, f32[1,8,4,128]{3,2,1,0:T(4,128)S(1)}, u32[]{:S(2)}, u32[]{:S(2)}) collective-permute-start(f32[1,8,4,128]{3,2,1,0:T(4,128)S(1)} %pad_maximum_fusion.6), channel_id=1, source_target_pairs={{1,0},{2,1},{3,2},{5,4},{6,5},{7,6},{9,8},{10,9},{11,10},{13,12},{... | collective-permute-start | bytes 49160 | tf_op jit(solution)/shard_map/while/body/eval_jaxpr/ppermute | solution.py:18
  187.1 1.7 copy-start
  263.7 14.2 %copy-start.3 = (f32[1,8,128,128]{3,2,1,0:T(8,128)S(1)}, f32[1,8,128,128]{3,2,1,0:T(8,128)}, u32[]{:S(2)}) copy-start(f32[1,8,128,128]{3,2,1,0:T(8,128)} %param.12) | copy-start | bytes 1572868
  266.5 12.3 %copy-start.5 = (f32[1,8,128,128]{3,2,1,0:T(8,128)}, f32[1,8,128,128]{3,2,1,0:T(8,128)S(1)}, u32[]{:S(2)}) copy-start(f32[1,8,128,128]{3,2,1,0:T(8,128)S(1)} %add.163) | copy-start | bytes 1572868
  266.5 11.4 %collective-permute-start.2 = (f32[8,128,128]{2,1,0:T(8,128)S(1)}, f32[8,128,128]{2,1,0:T(8,128)S(1)}, u32[]{:S(2)}, u32[]{:S(2)}) collective-permute-start(f32[8,128,128]{2,1,0:T(8,128)S(1)} %bitcast.111), channel_id=1, source_target_pairs={{0,4},{4,8},{8,12},{12,16},{16,20},{20,24},{24,28},{1,5},{5,9},{9,... | collective-permute-start | bytes 1572872 | tf_op jit(solution)/shard_map/ppermute | solution.py:31
Sparse Core Ops, SparseCore 0:
  11.0 54.4 all-reduce.5
  191.3 25.8 all-gather.1
where the time goes:
time: 288 us; the launch traced here: 286 us
  local copies, waits for them, and re-layouts  79.5 us (28%)
  waiting for transfers between devices  66.1 us (23%)
  starting transfers between devices  46.1 us (16%)
  other arithmetic  40.4 us (14%)
  matrix products  38 us (13%)
  between operations  14.3 us (5%)
    mul x12, other arithmetic, advance(): open_cells * (current + strength * diffusivity * laplace - 0.5 * transport)  35.6 us
    ppermute x12, waiting for transfers between devices, padded(): lax.ppermute(lax.slice_in_dim(block, 0, width, axis=dim), axis, backward)  30.8 us
    ppermute x12, starting transfers between devices, padded(): lax.ppermute(lax.slice_in_dim(block, block.shape[dim] - width, None, axis...  28.3 us
    all_gather x1, waiting for transfers between devices, on_device(): every_jump = lax.all_gather(coarse_jump, 'tm', axis=0, tiled=True)  26 us
    dot_general x10, matrix products, apply_coarse(): jnp.einsum('...tik,tlk->...til', mixed_x, matrix_y, precision=exact_preci...  24.6 us
    ppermute x12, starting transfers between devices, padded(): lax.ppermute(lax.slice_in_dim(block, 0, width, axis=dim), axis, backward)  15.5 us
    dot_general x10, matrix products, apply_coarse(): jnp.einsum('tij,...tjk->...tik', matrix_x, coarse_values, precision=exact...  13.5 us
    dynamic_update_slice x8, local copies, waits for them, and re-layouts, on_device(): last_state, history = lax.scan(sweep, first_coarse, every_jump)  13.4 us
  transfers between devices with their start and end apart: 27, of which 14 were waited for; matrix products, arithmetic and copies ran while one was open for 37% of the time, Pallas kernels for 0%

commit v1 on v0

--- a/solution.py
+++ b/solution.py
@@ -2,9 +2,27 @@
 import jax.numpy as jnp
 from jax import lax
 from jax.sharding import PartitionSpec as P
+from jax.lax import axis_index, axis_size, ppermute
 
 SUB = 12
 exact_precision = lax.Precision.HIGHEST
+
+
+def change_wires(local_array, along_axis):
+    n_chips = axis_size(along_axis)
+    stack_in = [(h, (h + 1) % n_chips) for h in range(n_chips)]
+    parts_seen = [(h, (h - 1) % n_chips) for h in range(n_chips)]
+    later, next_value = ([local_array], [local_array])
+    for _ in range(n_chips // 2):
+        later.append(ppermute(later[-1], axis_name=along_axis, perm=stack_in))
+    no = 0
+    while no < (n_chips - 1) // 2:
+        next_value.append(ppermute(next_value[-1], axis_name=along_axis, perm=parts_seen))
+        no += 1
+    frame_out = jnp.concatenate([*later[::-1], *next_value[1:]], axis=0)
+    return jnp.roll(
+        frame_out, (axis_index(along_axis) - n_chips // 2) * local_array.shape[0], axis=0
+    )
 
 
 def padded(block, sides, width):
@@ -81,7 +99,7 @@
     correction = fine_ends - prolong(apply_coarse(restrict(starts), coarse_x, coarse_y))
     coarse_jump = restrict(correction)
     first_coarse = spread(restrict(starts[0]), "tm", 0)
-    every_jump = lax.all_gather(coarse_jump, "tm", axis=0, tiled=True)
+    every_jump = change_wires(coarse_jump, "tm")
 
     def sweep(state_now, jump):
         return (apply_coarse(state_now, coarse_x, coarse_y) + jump, state_now)

time: 288 us -> 335 us (1.16)
  starting transfers between devices: 46.1 us -> 80.1 us
  waiting for transfers between devices: 66.1 us -> 81.4 us
  matrix products: 38 us -> 31.2 us
  local copies, waits for them, and re-layouts: 79.5 us -> 83.2 us
    psum x1, waiting for transfers between devices: 0.02 us -> 48.4 us  [spread(): return lax.psum(kept, axis)]
    ppermute x12, waiting for transfers between devices: 30.8 us -> 0.03 us  [padded(): lax.ppermute(lax.slice_in_dim(block, 0, width, axis=dim), axis, backward)]
    ppermute x12, starting transfers between devices: 28.3 us -> 54.6 us  [padded(): lax.ppermute(lax.slice_in_dim(block, block.shape[dim] - width, None, axis...]
    all_gather x1 -> x0, waiting for transfers between devices: 26 us -> none  [on_device(): every_jump = lax.all_gather(coarse_jump, 'tm', axis=0, tiled=True)]
    ppermute x0 -> x7, waiting for transfers between devices: none -> 23.5 us  [the longest x4 23.5 us: change_wires(): later.append(ppermute(later[-1], axis_name=along_axis, perm=stack_in))]
    ppermute x0 -> x7, starting transfers between devices: none -> 8.04 us  [the longest x3 7.98 us: change_wires(): ppermute(next_value[-1], axis_name=along_axis, perm=parts_seen)]
    dot_general x10, matrix products: 24.6 us -> 17.8 us  [apply_coarse(): jnp.einsum('...tik,tlk->...til', mixed_x, matrix_y, precision=exact_preci...]
  transfers between devices with their start and end apart: 27 -> 33, of which waited for: 14 -> 6; matrix products, arithmetic and copies ran while one was open for 37% -> 7% of each run, Pallas kernels for 0% -> 0%
where the time goes in v1:
time: 335 us; the launch traced here: 333 us
  local copies, waits for them, and re-layouts  83.2 us (25%)
  waiting for transfers between devices  81.4 us (24%)
  starting transfers between devices  80.1 us (24%)
  other arithmetic  41.1 us (12%)
  matrix products  31.2 us (9%)
  between operations  14.5 us (4%)
    ppermute x12, starting transfers between devices, padded(): lax.ppermute(lax.slice_in_dim(block, block.shape[dim] - width, None, axis...  54.6 us
    psum x1, waiting for transfers between devices, spread(): return lax.psum(kept, axis)  48.4 us
    mul x12, other arithmetic, advance(): open_cells * (current + strength * diffusivity * laplace - 0.5 * transport)  35 us
    ppermute x4, waiting for transfers between devices, change_wires(): later.append(ppermute(later[-1], axis_name=along_axis, perm=stack_in))  23.5 us
    dot_general x10, matrix products, apply_coarse(): jnp.einsum('...tik,tlk->...til', mixed_x, matrix_y, precision=exact_preci...  17.8 us
    ppermute x12, starting transfers between devices, padded(): lax.ppermute(lax.slice_in_dim(block, 0, width, axis=dim), axis, backward)  15.5 us
    dynamic_update_slice x8, local copies, waits for them, and re-layouts, on_device(): last_state, history = lax.scan(sweep, first_coarse, every_jump)  13.4 us
    dot_general x10, matrix products, apply_coarse(): jnp.einsum('tij,...tjk->...tik', matrix_x, coarse_values, precision=exact...  13.3 us
  transfers between devices with their start and end apart: 33, of which 6 were waited for; matrix products, arithmetic and copies ran while one was open for 7% of the time, Pallas kernels for 0%

profile of v1, /device:TPU:4, one launch (start us, length us, event | category | flops | bytes accessed | tf_op | source)
XLA Modules:
  0.0 332.6 jit_solution(1930930146000571336)
XLA Ops:
  8.6 1.7 slice.112
  17.4 166.1 %while.25 = (s32[]{:T(128)}, f32[1,8,128,128]{2,1,3,0:T(8,128)S(1)}, f32[8,128,128]{1,0,2:T(8,128)}, f32[12]{0:T(128)S(1)}, f32[8,128,128]{1,0,2:T(8,128)}, /*in...) while((s32[]{:T(128)}, ...), condition=%wide.region_2.3_spmd, body=%wide.region_1.2_spmd.sunk | while | flops 2710714 | bytes 10800029 | solution.py:98
  19.0 4.5 %collective-permute-start.1 = (f32[1,8,4,128]{3,2,1,0:T(4,128)S(1)}, f32[1,8,4,128]{3,2,1,0:T(4,128)S(1)}, u32[]{:S(2)}, u32[]{:S(2)}) collective-permute-start(f32[1,8,4,128]{3,2,1,0:T(4,128)S(1)} %pad_maximum_fusion.6), channel_id=1, source_target_pairs={{0,1},{1,2},{2,3},{4,5},{5,6},{6,7},{8,9},{9,10},{10,11},{12,13},{... | collective-permute-start | bytes 49160 | tf_op jit(solution)/shard_map/while/body/eval_jaxpr/ppermute | solution.py:33
  28.3 2.9 fusion.60
  32.8 4.5 %collective-permute-start.1 = (f32[1,8,4,128]{3,2,1,0:T(4,128)S(1)}, f32[1,8,4,128]{3,2,1,0:T(4,128)S(1)}, u32[]{:S(2)}, u32[]{:S(2)}) collective-permute-start(f32[1,8,4,128]{3,2,1,0:T(4,128)S(1)} %pad_maximum_fusion.6), channel_id=1, source_target_pairs={{0,1},{1,2},{2,3},{4,5},{5,6},{6,7},{8,9},{9,10},{10,11},{12,13},{... | collective-permute-start | bytes 49160 | tf_op jit(solution)/shard_map/while/body/eval_jaxpr/ppermute | solution.py:33
  42.1 2.9 fusion.60
  46.7 4.5 %collective-permute-start.1 = (f32[1,8,4,128]{3,2,1,0:T(4,128)S(1)}, f32[1,8,4,128]{3,2,1,0:T(4,128)S(1)}, u32[]{:S(2)}, u32[]{:S(2)}) collective-permute-start(f32[1,8,4,128]{3,2,1,0:T(4,128)S(1)} %pad_maximum_fusion.6), channel_id=1, source_target_pairs={{0,1},{1,2},{2,3},{4,5},{5,6},{6,7},{8,9},{9,10},{10,11},{12,13},{... | collective-permute-start | bytes 49160 | tf_op jit(solution)/shard_map/while/body/eval_jaxpr/ppermute | solution.py:33
  56.0 2.9 fusion.60
  60.5 4.5 %collective-permute-start.1 = (f32[1,8,4,128]{3,2,1,0:T(4,128)S(1)}, f32[1,8,4,128]{3,2,1,0:T(4,128)S(1)}, u32[]{:S(2)}, u32[]{:S(2)}) collective-permute-start(f32[1,8,4,128]{3,2,1,0:T(4,128)S(1)} %pad_maximum_fusion.6), channel_id=1, source_target_pairs={{0,1},{1,2},{2,3},{4,5},{5,6},{6,7},{8,9},{9,10},{10,11},{12,13},{... | collective-permute-start | bytes 49160 | tf_op jit(solution)/shard_map/while/body/eval_jaxpr/ppermute | solution.py:33
  69.8 2.9 fusion.60
  74.3 4.5 %collective-permute-start.1 = (f32[1,8,4,128]{3,2,1,0:T(4,128)S(1)}, f32[1,8,4,128]{3,2,1,0:T(4,128)S(1)}, u32[]{:S(2)}, u32[]{:S(2)}) collective-permute-start(f32[1,8,4,128]{3,2,1,0:T(4,128)S(1)} %pad_maximum_fusion.6), channel_id=1, source_target_pairs={{0,1},{1,2},{2,3},{4,5},{5,6},{6,7},{8,9},{9,10},{10,11},{12,13},{... | collective-permute-start | bytes 49160 | tf_op jit(solution)/shard_map/while/body/eval_jaxpr/ppermute | solution.py:33
  83.7 2.9 fusion.60
  88.2 4.5 %collective-permute-start.1 = (f32[1,8,4,128]{3,2,1,0:T(4,128)S(1)}, f32[1,8,4,128]{3,2,1,0:T(4,128)S(1)}, u32[]{:S(2)}, u32[]{:S(2)}) collective-permute-start(f32[1,8,4,128]{3,2,1,0:T(4,128)S(1)} %pad_maximum_fusion.6), channel_id=1, source_target_pairs={{0,1},{1,2},{2,3},{4,5},{5,6},{6,7},{8,9},{9,10},{10,11},{12,13},{... | collective-permute-start | bytes 49160 | tf_op jit(solution)/shard_map/while/body/eval_jaxpr/ppermute | solution.py:33
  97.5 2.9 fusion.60
  102.0 4.5 %collective-permute-start.1 = (f32[1,8,4,128]{3,2,1,0:T(4,128)S(1)}, f32[1,8,4,128]{3,2,1,0:T(4,128)S(1)}, u32[]{:S(2)}, u32[]{:S(2)}) collective-permute-start(f32[1,8,4,128]{3,2,1,0:T(4,128)S(1)} %pad_maximum_fusion.6), channel_id=1, source_target_pairs={{0,1},{1,2},{2,3},{4,5},{5,6},{6,7},{8,9},{9,10},{10,11},{12,13},{... | collective-permute-start | bytes 49160 | tf_op jit(solution)/shard_map/while/body/eval_jaxpr/ppermute | solution.py:33
  111.3 2.9 fusion.60
  115.9 4.5 %collective-permute-start.1 = (f32[1,8,4,128]{3,2,1,0:T(4,128)S(1)}, f32[1,8,4,128]{3,2,1,0:T(4,128)S(1)}, u32[]{:S(2)}, u32[]{:S(2)}) collective-permute-start(f32[1,8,4,128]{3,2,1,0:T(4,128)S(1)} %pad_maximum_fusion.6), channel_id=1, source_target_pairs={{0,1},{1,2},{2,3},{4,5},{5,6},{6,7},{8,9},{9,10},{10,11},{12,13},{... | collective-permute-start | bytes 49160 | tf_op jit(solution)/shard_map/while/body/eval_jaxpr/ppermute | solution.py:33
  125.2 2.9 fusion.60
  129.7 4.5 %collective-permute-start.1 = (f32[1,8,4,128]{3,2,1,0:T(4,128)S(1)}, f32[1,8,4,128]{3,2,1,0:T(4,128)S(1)}, u32[]{:S(2)}, u32[]{:S(2)}) collective-permute-start(f32[1,8,4,128]{3,2,1,0:T(4,128)S(1)} %pad_maximum_fusion.6), channel_id=1, source_target_pairs={{0,1},{1,2},{2,3},{4,5},{5,6},{6,7},{8,9},{9,10},{10,11},{12,13},{... | collective-permute-start | bytes 49160 | tf_op jit(solution)/shard_map/while/body/eval_jaxpr/ppermute | solution.py:33
  139.0 2.9 fusion.60
  143.5 4.5 %collective-permute-start.1 = (f32[1,8,4,128]{3,2,1,0:T(4,128)S(1)}, f32[1,8,4,128]{3,2,1,0:T(4,128)S(1)}, u32[]{:S(2)}, u32[]{:S(2)}) collective-permute-start(f32[1,8,4,128]{3,2,1,0:T(4,128)S(1)} %pad_maximum_fusion.6), channel_id=1, source_target_pairs={{0,1},{1,2},{2,3},{4,5},{5,6},{6,7},{8,9},{9,10},{10,11},{12,13},{... | collective-permute-start | bytes 49160 | tf_op jit(solution)/shard_map/while/body/eval_jaxpr/ppermute | solution.py:33
  152.9 2.9 fusion.60
  157.4 4.5 %collective-permute-start.1 = (f32[1,8,4,128]{3,2,1,0:T(4,128)S(1)}, f32[1,8,4,128]{3,2,1,0:T(4,128)S(1)}, u32[]{:S(2)}, u32[]{:S(2)}) collective-permute-start(f32[1,8,4,128]{3,2,1,0:T(4,128)S(1)} %pad_maximum_fusion.6), channel_id=1, source_target_pairs={{0,1},{1,2},{2,3},{4,5},{5,6},{6,7},{8,9},{9,10},{10,11},{12,13},{... | collective-permute-start | bytes 49160 | tf_op jit(solution)/shard_map/while/body/eval_jaxpr/ppermute | solution.py:33
  166.7 2.9 fusion.60
  171.2 4.5 %collective-permute-start.1 = (f32[1,8,4,128]{3,2,1,0:T(4,128)S(1)}, f32[1,8,4,128]{3,2,1,0:T(4,128)S(1)}, u32[]{:S(2)}, u32[]{:S(2)}) collective-permute-start(f32[1,8,4,128]{3,2,1,0:T(4,128)S(1)} %pad_maximum_fusion.6), channel_id=1, source_target_pairs={{0,1},{1,2},{2,3},{4,5},{5,6},{6,7},{8,9},{9,10},{10,11},{12,13},{... | collective-permute-start | bytes 49160 | tf_op jit(solution)/shard_map/while/body/eval_jaxpr/ppermute | solution.py:33
  180.5 2.9 fusion.60
  185.1 2.2 fusion.32
  187.9 6.7 %collective-permute-done.2 = f32[1,8,64,128]{3,2,1,0:T(8,128)S(1)} collective-permute-done((f32[1,8,64,128]{3,2,1,0:T(8,128)S(1)}, f32[1,8,64,128]{3,2,1,0:T(8,128)S(1)}, u32[]{:S(2)}, u32[]{:S(2)}) %collective-permute-start.2) | collective-permute-done | bytes 262176 | tf_op jit(solution)/shard_map/ppermute | solution.py:17
  194.6 2.6 collective-permute-start.6
  197.2 6.8 %collective-permute-done.3 = f32[1,8,64,128]{3,2,1,0:T(8,128)S(1)} collective-permute-done((f32[1,8,64,128]{3,2,1,0:T(8,128)S(1)}, f32[1,8,64,128]{3,2,1,0:T(8,128)S(1)}, u32[]{:S(2)}, u32[]{:S(2)}) %collective-permute-start.3) | collective-permute-done | bytes 262176 | tf_op jit(solution)/shard_map/ppermute | solution.py:17
  204.0 2.6 collective-permute-start.7
  206.7 5.9 %collective-permute-done.4 = f32[1,8,64,128]{3,2,1,0:T(8,128)S(1)} collective-permute-done((f32[1,8,64,128]{3,2,1,0:T(8,128)S(1)}, f32[1,8,64,128]{3,2,1,0:T(8,128)S(1)}, u32[]{:S(2)}, u32[]{:S(2)}) %collective-permute-start.4) | collective-permute-done | bytes 262176 | tf_op jit(solution)/shard_map/ppermute | solution.py:17
  213.5 1.7 multiply_select_fusion
  215.2 2.7 collective-permute-start.8
  217.9 4.1 %collective-permute-done.5 = f32[1,8,64,128]{3,2,1,0:T(8,128)S(1)} collective-permute-done((f32[1,8,64,128]{3,2,1,0:T(8,128)S(1)}, f32[1,8,64,128]{3,2,1,0:T(8,128)S(1)}, u32[]{:S(2)}, u32[]{:S(2)}) %collective-permute-start.5) | collective-permute-done | bytes 262176 | tf_op jit(solution)/shard_map/ppermute | solution.py:17
  222.8 48.4 %all-reduce.6.cloned.1.call-done = f32[8,64,128]{2,1,0:T(8,128)} async-done(((f32[8,64,128]{2,1,0:T(8,128)}), f32[8,64,128]{2,1,0:T(8,128)}) %all-reduce.6.cloned.1.call-update) | async-done | bytes 262160 | tf_op jit(solution)/shard_map/psum | solution.py:43
  271.2 38.6 %while.26 = (s32[]{:T(128)}, f32[8,64,128]{2,1,0:T(8,128)}, f32[8,8,64,128]{3,2,1,0:T(8,128)}, f32[8,64,64]{2,1,0:T(8,128)S(1)}, f32[8,128,128]{2,1,0:T(8,128)S(1)}, /*index=5*/f32[8,8,64,128]{3,2,1,0:T(8,128)S(1)}, s32[]{:T(128)}) while((s32[]{:T(128)}, f32[8,64,128]{2,1,0:T(8,128)}, f32[8,8,64,128]{3,2,1,0:T(8,128)}, ...), condition=%wide.region_4.5_spmd, body=%wide.region_3.4_spmd.sunk | while | flops 151060480 | bytes 2490961 | solution.py:107
  274.2 1.8 convolution_add_fusion.2
  279.0 1.8 convolution_add_fusion.2
  283.8 1.8 convolution_add_fusion.2
  288.6 1.8 convolution_add_fusion.2
  293.4 1.8 convolution_add_fusion.2
  298.3 1.8 convolution_add_fusion.2
  300.1 1.7 bitcast_dynamic-update-slice_fusion.2
  303.1 1.8 convolution_add_fusion.2
  307.9 1.8 convolution_add_fusion.2
  313.5 1.9 collective-permute-start.9
  315.4 9.5 %collective-permute-done.9 = f32[8,128,128]{2,1,0:T(8,128)S(1)} collective-permute-done((f32[8,128,128]{2,1,0:T(8,128)S(1)}, f32[8,128,128]{2,1,0:T(8,128)S(1)}, u32[]{:S(2)}, u32[]{:S(2)}) %collective-permute-start.9) | collective-permute-done | bytes 524320 | tf_op jit(solution)/shard_map/ppermute | solution.py:49
  (311 shorter events, 114.4 us)
Async XLA Ops:
  7.2 8.1 %copy-start.5 = (s32[8,128,128]{2,1,0:T(8,128)S(1)}, s32[8,128,128]{2,1,0:T(8,128)}, u32[]{:S(2)}) copy-start(s32[8,128,128]{2,1,0:T(8,128)} %param.15) | copy-start | bytes 1572868
  7.2 264.0 %all-reduce.6.cloned.1.call-start = ((), (), s32[]{:S(2)}) async-start(), calls=%async_computation | async-start | bytes 524288 | tf_op jit(solution)/shard_map/psum | solution.py:43
  7.2 9.1 %copy-start.6 = (f32[8,128,128]{2,1,0:T(8,128)S(1)}, f32[8,128,128]{2,1,0:T(8,128)}, u32[]{:S(2)}) copy-start(f32[8,128,128]{2,1,0:T(8,128)} %param.13) | copy-start | bytes 1572868
  8.6 8.8 %copy-start.7 = (s32[8,4]{0,1:T(4,128)S(1)}, s32[8,4]{0,1:T(4,128)}, u32[]{:S(2)}) copy-start(s32[8,4]{0,1:T(4,128)} %param.17) | copy-start | bytes 388
  8.6 8.8 %copy-start.8 = (f32[12]{0:T(128)S(1)}, f32[12]{0:T(128)}, u32[]{:S(2)}) copy-start(f32[12]{0:T(128)} %param.16) | copy-start | bytes 148
  17.4 166.3 %copy-start.1 = (f32[8,64,64]{2,1,0:T(8,128)S(1)}, f32[8,64,64]{2,1,0:T(8,128)}, u32[]{:S(2)}) copy-start(f32[8,64,64]{2,1,0:T(8,128)} %param.18) | copy-start | bytes 393220
  17.7 7.6 %collective-permute-start = (f32[1,8,4,128]{3,2,1,0:T(4,128)S(1)}, f32[1,8,4,128]{3,2,1,0:T(4,128)S(1)}, u32[]{:S(2)}, u32[]{:S(2)}) collective-permute-start(f32[1,8,4,128]{3,2,1,0:T(4,128)S(1)} %pad_maximum_fusion.6), channel_id=1, source_target_pairs={{1,0},{2,1},{3,2},{5,4},{6,5},{7,6},{9,8},{10,9},{11,10},{13,12},{... | collective-permute-start | bytes 49160 | tf_op jit(solution)/shard_map/while/body/eval_jaxpr/ppermute | solution.py:36
  19.0 6.3 %collective-permute-start.1 = (f32[1,8,4,128]{3,2,1,0:T(4,128)S(1)}, f32[1,8,4,128]{3,2,1,0:T(4,128)S(1)}, u32[]{:S(2)}, u32[]{:S(2)}) collective-permute-start(f32[1,8,4,128]{3,2,1,0:T(4,128)S(1)} %pad_maximum_fusion.6), channel_id=1, source_target_pairs={{0,1},{1,2},{2,3},{4,5},{5,6},{6,7},{8,9},{9,10},{10,11},{12,13},{... | collective-permute-start | bytes 49160 | tf_op jit(solution)/shard_map/while/body/eval_jaxpr/ppermute | solution.py:33
  31.5 7.6 %collective-permute-start = (f32[1,8,4,128]{3,2,1,0:T(4,128)S(1)}, f32[1,8,4,128]{3,2,1,0:T(4,128)S(1)}, u32[]{:S(2)}, u32[]{:S(2)}) collective-permute-start(f32[1,8,4,128]{3,2,1,0:T(4,128)S(1)} %pad_maximum_fusion.6), channel_id=1, source_target_pairs={{1,0},{2,1},{3,2},{5,4},{6,5},{7,6},{9,8},{10,9},{11,10},{13,12},{... | collective-permute-start | bytes 49160 | tf_op jit(solution)/shard_map/while/body/eval_jaxpr/ppermute | solution.py:36
  32.8 6.3 %collective-permute-start.1 = (f32[1,8,4,128]{3,2,1,0:T(4,128)S(1)}, f32[1,8,4,128]{3,2,1,0:T(4,128)S(1)}, u32[]{:S(2)}, u32[]{:S(2)}) collective-permute-start(f32[1,8,4,128]{3,2,1,0:T(4,128)S(1)} %pad_maximum_fusion.6), channel_id=1, source_target_pairs={{0,1},{1,2},{2,3},{4,5},{5,6},{6,7},{8,9},{9,10},{10,11},{12,13},{... | collective-permute-start | bytes 49160 | tf_op jit(solution)/shard_map/while/body/eval_jaxpr/ppermute | solution.py:33
  45.4 7.6 %collective-permute-start = (f32[1,8,4,128]{3,2,1,0:T(4,128)S(1)}, f32[1,8,4,128]{3,2,1,0:T(4,128)S(1)}, u32[]{:S(2)}, u32[]{:S(2)}) collective-permute-start(f32[1,8,4,128]{3,2,1,0:T(4,128)S(1)} %pad_maximum_fusion.6), channel_id=1, source_target_pairs={{1,0},{2,1},{3,2},{5,4},{6,5},{7,6},{9,8},{10,9},{11,10},{13,12},{... | collective-permute-start | bytes 49160 | tf_op jit(solution)/shard_map/while/body/eval_jaxpr/ppermute | solution.py:36
  46.7 6.3 %collective-permute-start.1 = (f32[1,8,4,128]{3,2,1,0:T(4,128)S(1)}, f32[1,8,4,128]{3,2,1,0:T(4,128)S(1)}, u32[]{:S(2)}, u32[]{:S(2)}) collective-permute-start(f32[1,8,4,128]{3,2,1,0:T(4,128)S(1)} %pad_maximum_fusion.6), channel_id=1, source_target_pairs={{0,1},{1,2},{2,3},{4,5},{5,6},{6,7},{8,9},{9,10},{10,11},{12,13},{... | collective-permute-start | bytes 49160 | tf_op jit(solution)/shard_map/while/body/eval_jaxpr/ppermute | solution.py:33
  59.2 7.6 %collective-permute-start = (f32[1,8,4,128]{3,2,1,0:T(4,128)S(1)}, f32[1,8,4,128]{3,2,1,0:T(4,128)S(1)}, u32[]{:S(2)}, u32[]{:S(2)}) collective-permute-start(f32[1,8,4,128]{3,2,1,0:T(4,128)S(1)} %pad_maximum_fusion.6), channel_id=1, source_target_pairs={{1,0},{2,1},{3,2},{5,4},{6,5},{7,6},{9,8},{10,9},{11,10},{13,12},{... | collective-permute-start | bytes 49160 | tf_op jit(solution)/shard_map/while/body/eval_jaxpr/ppermute | solution.py:36
  60.5 6.3 %collective-permute-start.1 = (f32[1,8,4,128]{3,2,1,0:T(4,128)S(1)}, f32[1,8,4,128]{3,2,1,0:T(4,128)S(1)}, u32[]{:S(2)}, u32[]{:S(2)}) collective-permute-start(f32[1,8,4,128]{3,2,1,0:T(4,128)S(1)} %pad_maximum_fusion.6), channel_id=1, source_target_pairs={{0,1},{1,2},{2,3},{4,5},{5,6},{6,7},{8,9},{9,10},{10,11},{12,13},{... | collective-permute-start | bytes 49160 | tf_op jit(solution)/shard_map/while/body/eval_jaxpr/ppermute | solution.py:33
  73.0 7.6 %collective-permute-start = (f32[1,8,4,128]{3,2,1,0:T(4,128)S(1)}, f32[1,8,4,128]{3,2,1,0:T(4,128)S(1)}, u32[]{:S(2)}, u32[]{:S(2)}) collective-permute-start(f32[1,8,4,128]{3,2,1,0:T(4,128)S(1)} %pad_maximum_fusion.6), channel_id=1, source_target_pairs={{1,0},{2,1},{3,2},{5,4},{6,5},{7,6},{9,8},{10,9},{11,10},{13,12},{... | collective-permute-start | bytes 49160 | tf_op jit(solution)/shard_map/while/body/eval_jaxpr/ppermute | solution.py:36
  74.3 6.3 %collective-permute-start.1 = (f32[1,8,4,128]{3,2,1,0:T(4,128)S(1)}, f32[1,8,4,128]{3,2,1,0:T(4,128)S(1)}, u32[]{:S(2)}, u32[]{:S(2)}) collective-permute-start(f32[1,8,4,128]{3,2,1,0:T(4,128)S(1)} %pad_maximum_fusion.6), channel_id=1, source_target_pairs={{0,1},{1,2},{2,3},{4,5},{5,6},{6,7},{8,9},{9,10},{10,11},{12,13},{... | collective-permute-start | bytes 49160 | tf_op jit(solution)/shard_map/while/body/eval_jaxpr/ppermute | solution.py:33
  86.9 7.6 %collective-permute-start = (f32[1,8,4,128]{3,2,1,0:T(4,128)S(1)}, f32[1,8,4,128]{3,2,1,0:T(4,128)S(1)}, u32[]{:S(2)}, u32[]{:S(2)}) collective-permute-start(f32[1,8,4,128]{3,2,1,0:T(4,128)S(1)} %pad_maximum_fusion.6), channel_id=1, source_target_pairs={{1,0},{2,1},{3,2},{5,4},{6,5},{7,6},{9,8},{10,9},{11,10},{13,12},{... | collective-permute-start | bytes 49160 | tf_op jit(solution)/shard_map/while/body/eval_jaxpr/ppermute | solution.py:36
  88.2 6.3 %collective-permute-start.1 = (f32[1,8,4,128]{3,2,1,0:T(4,128)S(1)}, f32[1,8,4,128]{3,2,1,0:T(4,128)S(1)}, u32[]{:S(2)}, u32[]{:S(2)}) collective-permute-start(f32[1,8,4,128]{3,2,1,0:T(4,128)S(1)} %pad_maximum_fusion.6), channel_id=1, source_target_pairs={{0,1},{1,2},{2,3},{4,5},{5,6},{6,7},{8,9},{9,10},{10,11},{12,13},{... | collective-permute-start | bytes 49160 | tf_op jit(solution)/shard_map/while/body/eval_jaxpr/ppermute | solution.py:33
  100.7 7.6 %collective-permute-start = (f32[1,8,4,128]{3,2,1,0:T(4,128)S(1)}, f32[1,8,4,128]{3,2,1,0:T(4,128)S(1)}, u32[]{:S(2)}, u32[]{:S(2)}) collective-permute-start(f32[1,8,4,128]{3,2,1,0:T(4,128)S(1)} %pad_maximum_fusion.6), channel_id=1, source_target_pairs={{1,0},{2,1},{3,2},{5,4},{6,5},{7,6},{9,8},{10,9},{11,10},{13,12},{... | collective-permute-start | bytes 49160 | tf_op jit(solution)/shard_map/while/body/eval_jaxpr/ppermute | solution.py:36
  102.0 6.3 %collective-permute-start.1 = (f32[1,8,4,128]{3,2,1,0:T(4,128)S(1)}, f32[1,8,4,128]{3,2,1,0:T(4,128)S(1)}, u32[]{:S(2)}, u32[]{:S(2)}) collective-permute-start(f32[1,8,4,128]{3,2,1,0:T(4,128)S(1)} %pad_maximum_fusion.6), channel_id=1, source_target_pairs={{0,1},{1,2},{2,3},{4,5},{5,6},{6,7},{8,9},{9,10},{10,11},{12,13},{... | collective-permute-start | bytes 49160 | tf_op jit(solution)/shard_map/while/body/eval_jaxpr/ppermute | solution.py:33
  114.6 7.6 %collective-permute-start = (f32[1,8,4,128]{3,2,1,0:T(4,128)S(1)}, f32[1,8,4,128]{3,2,1,0:T(4,128)S(1)}, u32[]{:S(2)}, u32[]{:S(2)}) collective-permute-start(f32[1,8,4,128]{3,2,1,0:T(4,128)S(1)} %pad_maximum_fusion.6), channel_id=1, source_target_pairs={{1,0},{2,1},{3,2},{5,4},{6,5},{7,6},{9,8},{10,9},{11,10},{13,12},{... | collective-permute-start | bytes 49160 | tf_op jit(solution)/shard_map/while/body/eval_jaxpr/ppermute | solution.py:36
  115.9 6.3 %collective-permute-start.1 = (f32[1,8,4,128]{3,2,1,0:T(4,128)S(1)}, f32[1,8,4,128]{3,2,1,0:T(4,128)S(1)}, u32[]{:S(2)}, u32[]{:S(2)}) collective-permute-start(f32[1,8,4,128]{3,2,1,0:T(4,128)S(1)} %pad_maximum_fusion.6), channel_id=1, source_target_pairs={{0,1},{1,2},{2,3},{4,5},{5,6},{6,7},{8,9},{9,10},{10,11},{12,13},{... | collective-permute-start | bytes 49160 | tf_op jit(solution)/shard_map/while/body/eval_jaxpr/ppermute | solution.py:33
  128.4 7.6 %collective-permute-start = (f32[1,8,4,128]{3,2,1,0:T(4,128)S(1)}, f32[1,8,4,128]{3,2,1,0:T(4,128)S(1)}, u32[]{:S(2)}, u32[]{:S(2)}) collective-permute-start(f32[1,8,4,128]{3,2,1,0:T(4,128)S(1)} %pad_maximum_fusion.6), channel_id=1, source_target_pairs={{1,0},{2,1},{3,2},{5,4},{6,5},{7,6},{9,8},{10,9},{11,10},{13,12},{... | collective-permute-start | bytes 49160 | tf_op jit(solution)/shard_map/while/body/eval_jaxpr/ppermute | solution.py:36
  129.7 6.3 %collective-permute-start.1 = (f32[1,8,4,128]{3,2,1,0:T(4,128)S(1)}, f32[1,8,4,128]{3,2,1,0:T(4,128)S(1)}, u32[]{:S(2)}, u32[]{:S(2)}) collective-permute-start(f32[1,8,4,128]{3,2,1,0:T(4,128)S(1)} %pad_maximum_fusion.6), channel_id=1, source_target_pairs={{0,1},{1,2},{2,3},{4,5},{5,6},{6,7},{8,9},{9,10},{10,11},{12,13},{... | collective-permute-start | bytes 49160 | tf_op jit(solution)/shard_map/while/body/eval_jaxpr/ppermute | solution.py:33
  142.2 7.6 %collective-permute-start = (f32[1,8,4,128]{3,2,1,0:T(4,128)S(1)}, f32[1,8,4,128]{3,2,1,0:T(4,128)S(1)}, u32[]{:S(2)}, u32[]{:S(2)}) collective-permute-start(f32[1,8,4,128]{3,2,1,0:T(4,128)S(1)} %pad_maximum_fusion.6), channel_id=1, source_target_pairs={{1,0},{2,1},{3,2},{5,4},{6,5},{7,6},{9,8},{10,9},{11,10},{13,12},{... | collective-permute-start | bytes 49160 | tf_op jit(solution)/shard_map/while/body/eval_jaxpr/ppermute | solution.py:36
  143.5 6.3 %collective-permute-start.1 = (f32[1,8,4,128]{3,2,1,0:T(4,128)S(1)}, f32[1,8,4,128]{3,2,1,0:T(4,128)S(1)}, u32[]{:S(2)}, u32[]{:S(2)}) collective-permute-start(f32[1,8,4,128]{3,2,1,0:T(4,128)S(1)} %pad_maximum_fusion.6), channel_id=1, source_target_pairs={{0,1},{1,2},{2,3},{4,5},{5,6},{6,7},{8,9},{9,10},{10,11},{12,13},{... | collective-permute-start | bytes 49160 | tf_op jit(solution)/shard_map/while/body/eval_jaxpr/ppermute | solution.py:33
  156.1 7.6 %collective-permute-start = (f32[1,8,4,128]{3,2,1,0:T(4,128)S(1)}, f32[1,8,4,128]{3,2,1,0:T(4,128)S(1)}, u32[]{:S(2)}, u32[]{:S(2)}) collective-permute-start(f32[1,8,4,128]{3,2,1,0:T(4,128)S(1)} %pad_maximum_fusion.6), channel_id=1, source_target_pairs={{1,0},{2,1},{3,2},{5,4},{6,5},{7,6},{9,8},{10,9},{11,10},{13,12},{... | collective-permute-start | bytes 49160 | tf_op jit(solution)/shard_map/while/body/eval_jaxpr/ppermute | solution.py:36
  157.4 6.3 %collective-permute-start.1 = (f32[1,8,4,128]{3,2,1,0:T(4,128)S(1)}, f32[1,8,4,128]{3,2,1,0:T(4,128)S(1)}, u32[]{:S(2)}, u32[]{:S(2)}) collective-permute-start(f32[1,8,4,128]{3,2,1,0:T(4,128)S(1)} %pad_maximum_fusion.6), channel_id=1, source_target_pairs={{0,1},{1,2},{2,3},{4,5},{5,6},{6,7},{8,9},{9,10},{10,11},{12,13},{... | collective-permute-start | bytes 49160 | tf_op jit(solution)/shard_map/while/body/eval_jaxpr/ppermute | solution.py:33
  169.9 7.6 %collective-permute-start = (f32[1,8,4,128]{3,2,1,0:T(4,128)S(1)}, f32[1,8,4,128]{3,2,1,0:T(4,128)S(1)}, u32[]{:S(2)}, u32[]{:S(2)}) collective-permute-start(f32[1,8,4,128]{3,2,1,0:T(4,128)S(1)} %pad_maximum_fusion.6), channel_id=1, source_target_pairs={{1,0},{2,1},{3,2},{5,4},{6,5},{7,6},{9,8},{10,9},{11,10},{13,12},{... | collective-permute-start | bytes 49160 | tf_op jit(solution)/shard_map/while/body/eval_jaxpr/ppermute | solution.py:36
  171.2 6.3 %collective-permute-start.1 = (f32[1,8,4,128]{3,2,1,0:T(4,128)S(1)}, f32[1,8,4,128]{3,2,1,0:T(4,128)S(1)}, u32[]{:S(2)}, u32[]{:S(2)}) collective-permute-start(f32[1,8,4,128]{3,2,1,0:T(4,128)S(1)} %pad_maximum_fusion.6), channel_id=1, source_target_pairs={{0,1},{1,2},{2,3},{4,5},{5,6},{6,7},{8,9},{9,10},{10,11},{12,13},{... | collective-permute-start | bytes 49160 | tf_op jit(solution)/shard_map/while/body/eval_jaxpr/ppermute | solution.py:33
  183.5 29.1 %copy-start.2 = (f32[1,8,128,128]{3,2,1,0:T(8,128)S(1)}, f32[1,8,128,128]{3,2,1,0:T(8,128)}, u32[]{:S(2)}) copy-start(f32[1,8,128,128]{3,2,1,0:T(8,128)} %param.12) | copy-start | bytes 1572868
  187.6 34.7 %copy-start.3 = (f32[1,8,128,128]{3,2,1,0:T(8,128)}, f32[1,8,128,128]{3,2,1,0:T(8,128)S(1)}, u32[]{:S(2)}) copy-start(f32[1,8,128,128]{3,2,1,0:T(8,128)S(1)} %sub.73) | copy-start | bytes 1572868
  187.9 6.7 %collective-permute-start.2 = (f32[1,8,64,128]{3,2,1,0:T(8,128)S(1)}, f32[1,8,64,128]{3,2,1,0:T(8,128)S(1)}, u32[]{:S(2)}, u32[]{:S(2)}) collective-permute-start(f32[1,8,64,128]{3,2,1,0:T(8,128)S(1)} %add_multiply_fusion), channel_id=1, source_target_pairs={{0,4},{4,8},{8,12},{12,16},{16,20},{20,24},{24,28},{28,0},{1,5},{5... | collective-permute-start | bytes 786440 | tf_op jit(solution)/shard_map/ppermute | solution.py:17
  194.6 9.4 %collective-permute-start.3 = (f32[1,8,64,128]{3,2,1,0:T(8,128)S(1)}, f32[1,8,64,128]{3,2,1,0:T(8,128)S(1)}, u32[]{:S(2)}, u32[]{:S(2)}) collective-permute-start(f32[1,8,64,128]{3,2,1,0:T(8,128)S(1)} %collective-permute-done.2), channel_id=1, source_target_pairs={{0,4},{4,8},{8,12},{12,16},{16,20},{20,24},{24,28},{28,0},{1,5},{5... | collective-permute-start | bytes 786440 | tf_op jit(solution)/shard_map/ppermute | solution.py:17
  194.6 9.4 %collective-permute-start.6 = (f32[1,8,64,128]{3,2,1,0:T(8,128)S(1)}, f32[1,8,64,128]{3,2,1,0:T(8,128)S(1)}, u32[]{:S(2)}, u32[]{:S(2)}) collective-permute-start(f32[1,8,64,128]{3,2,1,0:T(8,128)S(1)} %add_multiply_fusion), channel_id=1, source_target_pairs={{0,28},{4,0},{8,4},{12,8},{16,12},{20,16},{24,20},{28,24},{1,29},{... | collective-permute-start | bytes 786440 | tf_op jit(solution)/shard_map/ppermute | solution.py:20
  204.0 8.5 %collective-permute-start.4 = (f32[1,8,64,128]{3,2,1,0:T(8,128)S(1)}, f32[1,8,64,128]{3,2,1,0:T(8,128)S(1)}, u32[]{:S(2)}, u32[]{:S(2)}) collective-permute-start(f32[1,8,64,128]{3,2,1,0:T(8,128)S(1)} %collective-permute-done.3), channel_id=1, source_target_pairs={{0,4},{4,8},{8,12},{12,16},{16,20},{20,24},{24,28},{28,0},{1,5},{5... | collective-permute-start | bytes 786440 | tf_op jit(solution)/shard_map/ppermute | solution.py:17
  204.0 11.2 %collective-permute-start.7 = (f32[1,8,64,128]{3,2,1,0:T(8,128)S(1)}, f32[1,8,64,128]{3,2,1,0:T(8,128)S(1)}, u32[]{:S(2)}, u32[]{:S(2)}) collective-permute-start(f32[1,8,64,128]{3,2,1,0:T(8,128)S(1)} %collective-permute-done.6), channel_id=1, source_target_pairs={{0,28},{4,0},{8,4},{12,8},{16,12},{20,16},{24,20},{28,24},{1,29},{... | collective-permute-start | bytes 786440 | tf_op jit(solution)/shard_map/ppermute | solution.py:20
  212.6 9.5 %collective-permute-start.5 = (f32[1,8,64,128]{3,2,1,0:T(8,128)S(1)}, f32[1,8,64,128]{3,2,1,0:T(8,128)S(1)}, u32[]{:S(2)}, u32[]{:S(2)}) collective-permute-start(f32[1,8,64,128]{3,2,1,0:T(8,128)S(1)} %collective-permute-done.4), channel_id=1, source_target_pairs={{0,4},{4,8},{8,12},{12,16},{16,20},{20,24},{24,28},{28,0},{1,5},{5... | collective-permute-start | bytes 786440 | tf_op jit(solution)/shard_map/ppermute | solution.py:17
  215.2 7.0 %collective-permute-start.8 = (f32[1,8,64,128]{3,2,1,0:T(8,128)S(1)}, f32[1,8,64,128]{3,2,1,0:T(8,128)S(1)}, u32[]{:S(2)}, u32[]{:S(2)}) collective-permute-start(f32[1,8,64,128]{3,2,1,0:T(8,128)S(1)} %collective-permute-done.7), channel_id=1, source_target_pairs={{0,28},{4,0},{8,4},{12,8},{16,12},{20,16},{24,20},{28,24},{1,29},{... | collective-permute-start | bytes 786440 | tf_op jit(solution)/shard_map/ppermute | solution.py:20
  222.3 48.9 %copy-start = (f32[8,128,128]{2,1,0:T(8,128)S(1)}, f32[8,128,128]{2,1,0:T(8,128)}, u32[]{:S(2)}) copy-start(f32[8,128,128]{2,1,0:T(8,128)} %param.19) | copy-start | bytes 1572868
  313.5 12.3 %copy-start.4 = (f32[1,8,128,128]{3,2,1,0:T(8,128)}, f32[1,8,128,128]{3,2,1,0:T(8,128)S(1)}, u32[]{:S(2)}) copy-start(f32[1,8,128,128]{3,2,1,0:T(8,128)S(1)} %add.176) | copy-start | bytes 1572868
  313.5 11.4 %collective-permute-start.9 = (f32[8,128,128]{2,1,0:T(8,128)S(1)}, f32[8,128,128]{2,1,0:T(8,128)S(1)}, u32[]{:S(2)}, u32[]{:S(2)}) collective-permute-start(f32[8,128,128]{2,1,0:T(8,128)S(1)} %bitcast.111), channel_id=1, source_target_pairs={{0,4},{4,8},{8,12},{12,16},{16,20},{20,24},{24,28},{1,5},{5,9},{9,... | collective-permute-start | bytes 1572872 | tf_op jit(solution)/shard_map/ppermute | solution.py:49
Sparse Core Ops, SparseCore 0:
  215.3 55.8 all-reduce.5
